TPU v7x, 32 devices: a whole 2x2x4 slice. The times are simulated.
32 devices in a mesh: groups: 2 (over y), req: 4 (over z), head: 2 (over x), sub: 2 (over core).
Axes of the slice: x: 2, y: 2, z: 4, core: 2. Of those that a mesh axis runs over, the one named last changes fastest.
Arguments:
- hidden_in: bfloat16 [1024, 8192], P(('groups', 'req')), parts along dimension 0, may hold values from -3 to 3
- q_weight: bfloat16 [8192, 8192], P('req', ('head', 'sub')), may hold values from -0.0625 to 0.0625
- q_gain: float32 [128], replicated, may hold values from 0.1 to 1.9
- key_cache: bfloat16 [8, 1601, 1024], P(('groups', 'req'), None, 'head'), parts along dimension 0, may hold values from -64 to 64
- value_cache: bfloat16 [8, 1601, 1024], P(('groups', 'req'), None, 'head'), parts along dimension 0, may hold values from -8 to 8
- out_weight: bfloat16 [8192, 8192], P(('head', 'sub'), 'req'), may hold values from -0.09375 to 0.09375
- req_image: int32 [1024], P(('groups', 'req')), parts along dimension 0, may hold values from 0 to 3, as said below
- image_count: int32 [1024], P(('groups', 'req')), parts along dimension 0, may hold values from 0 to 1, as said below
- image_home: int32 [8], P('groups'), parts along dimension 0, may hold values from 0 to 3, as said below
Outputs:
- layer_out: bfloat16 [1024, 8192], P(('groups', 'req'), ('head', 'sub')), parts along dimension 0
There are 2 independent parts, one for each index of `groups`. A program takes and returns all parts, laid end to end along the dimension named above; an argument that names none is the same for every part. Nothing has to cross between parts.
Inputs may be any that keep to these rules, and one draw needn't show every extreme that they name: Requests with image_count 0 attend to nothing; in each aligned block of 128 requests at most a quarter have image_count 0. In each aligned block of 128 requests, at most 64 requests with image_count 1 have one and the same value of image_home[req_image]; in every block exactly 64 of them share one value, and that value is the same for all blocks. `image_home`: each cache row holds exactly one image.
All inputs are finite; a program needn't handle non-finite values.
Results may differ from a plain program's by a relative error of at most 0.025.
Values may be sent and summed in bfloat16 or wider, within the bound.
No kernel may reach another device: no remote copies, remote signals or barrier semaphores. Data moves between devices by JAX's collectives and lax.ppermute only.
A program may use at most 128 MiB of HBM per device.

v0:
```python
import jax
import jax.numpy as jnp
from jax import lax
from jax.sharding import PartitionSpec as P

HQ = 64
KVH = 8


def normalize_heads(queries, q_gain, head_dim):
    row_count = queries.shape[0]
    per_head = queries.astype(jnp.float32).reshape(row_count, -1, head_dim)
    inv_rms = lax.rsqrt(jnp.mean(per_head * per_head, axis=2, keepdims=True) + 1e-05)
    return (per_head * inv_rms * q_gain).reshape(row_count, -1).astype(jnp.bfloat16)


def exchange_sum(parts, axis, count, index):
    total = lax.dynamic_index_in_dim(parts, index, axis=0, keepdims=False).astype(jnp.float32)
    for shift in range(1, count):
        outgoing = lax.dynamic_index_in_dim(parts, (index + shift) % count, axis=0, keepdims=False)
        incoming = lax.ppermute(outgoing, axis, [(i, (i + shift) % count) for i in range(count)])
        total = total + incoming.astype(jnp.float32)
    return total.astype(jnp.bfloat16)


def local(
    hidden_in,
    q_weight,
    q_gain,
    key_cache,
    value_cache,
    out_weight,
    req_image,
    image_count,
    image_home,
):
    req_count = lax.axis_size("req")
    local_rows = hidden_in.shape[0]
    q_cols = q_weight.shape[1]
    head_dim = q_gain.shape[0]
    group_size = HQ // KVH
    heads_here = q_cols // head_dim
    sub_count = lax.axis_size("sub")
    sub_index = lax.axis_index("sub")
    block_width = hidden_in.shape[1] // req_count
    part_width = block_width // sub_count
    by_block = hidden_in.reshape(local_rows, req_count, sub_count, part_width)
    my_part = lax.dynamic_index_in_dim(by_block, sub_index, axis=2, keepdims=False)
    spread_part = lax.all_to_all(my_part, "req", split_axis=1, concat_axis=0, tiled=True)
    spread_part = spread_part.reshape(req_count * local_rows, part_width)
    spread_cols = jnp.zeros((req_count * local_rows, block_width), spread_part.dtype)
    spread_cols = lax.dynamic_update_slice_in_dim(
        spread_cols, spread_part, sub_index * part_width, 1
    )
    for shift in range(1, sub_count):
        other_part = lax.ppermute(
            spread_part, "sub", [(i, (i + shift) % sub_count) for i in range(sub_count)]
        )
        spread_cols = lax.dynamic_update_slice_in_dim(
            spread_cols, other_part, (sub_index - shift) % sub_count * part_width, 1
        )
    query_sum = lax.psum_scatter(
        jnp.dot(spread_cols, q_weight, preferred_element_type=jnp.float32).astype(jnp.bfloat16),
        "req",
        scatter_dimension=0,
        tiled=True,
    )
    queries = lax.optimization_barrier(query_sum)
    normalized = normalize_heads(queries, q_gain, head_dim)
    capacity = 2 * local_rows // req_count
    slot_total = req_count * capacity
    table_ids = lax.broadcasted_iota(jnp.int32, (local_rows, image_home.shape[0]), 1)
    home_rows = jnp.sum(jnp.where(req_image[:, None] == table_ids, image_home[None, :], 0), axis=1)
    wanted = image_count == 1
    dest_ids = lax.broadcasted_iota(jnp.int32, (local_rows, req_count), 1)
    to_dest = ((home_rows[:, None] == dest_ids) & wanted[:, None]).astype(jnp.int32)
    earlier = jnp.cumsum(to_dest, axis=0) - to_dest
    position = home_rows * capacity + jnp.sum(earlier * to_dest, axis=1)
    slot_ids = lax.broadcasted_iota(jnp.int32, (slot_total, local_rows), 0)
    dispatch = ((slot_ids == position[None, :]) & wanted[None, :]).astype(jnp.bfloat16)
    outgoing = jnp.dot(dispatch, normalized, preferred_element_type=jnp.float32).astype(
        jnp.bfloat16
    )
    outgoing = outgoing.reshape(req_count, capacity, q_cols)
    kv_count = max(1, heads_here // group_size)
    per_kv = heads_here // kv_count
    kv_first = sub_index * heads_here // group_size
    keys_here = lax.dynamic_slice_in_dim(
        key_cache[0], kv_first * head_dim, kv_count * head_dim, 1
    ).reshape(-1, kv_count, head_dim)
    values_here = lax.dynamic_slice_in_dim(
        value_cache[0], kv_first * head_dim, kv_count * head_dim, 1
    ).reshape(-1, kv_count, head_dim)
    score_scale = head_dim ** (-0.5)
    arrived = lax.all_to_all(outgoing, "req", split_axis=0, concat_axis=0, tiled=True)
    sources = arrived.shape[0]
    slot_count = arrived.shape[1]
    flat_rows = arrived.reshape(sources * slot_count, kv_count, per_kv, head_dim)
    scores = (
        jnp.einsum("mkgd,tkd->kgmt", flat_rows, keys_here, preferred_element_type=jnp.float32)
        * score_scale
    )
    row_peak = jnp.max(scores, axis=3, keepdims=True)
    weights = jnp.exp(scores - row_peak)
    probs = (weights / jnp.sum(weights, axis=3, keepdims=True)).astype(jnp.bfloat16)
    mixed_heads = jnp.einsum(
        "kgmt,tkd->mkgd", probs, values_here, preferred_element_type=jnp.float32
    )
    replies = mixed_heads.astype(jnp.bfloat16).reshape(sources, slot_count, q_cols)
    returned = lax.all_to_all(replies, "req", split_axis=0, concat_axis=0, tiled=True)
    attended = lax.dot_general(
        dispatch,
        returned.reshape(slot_total, q_cols),
        (((0,), (0,)), ((), ())),
        preferred_element_type=jnp.float32,
    ).astype(jnp.bfloat16)
    partial_cols = jnp.dot(
        lax.all_gather(attended, "req", axis=0, tiled=True),
        out_weight,
        preferred_element_type=jnp.float32,
    ).astype(jnp.bfloat16)
    hs_count = lax.axis_size("head") * sub_count
    hs_index = lax.axis_index("head") * sub_count + sub_index
    req_index = lax.axis_index("req")
    head_count = lax.axis_size("head")
    by_group = partial_cols.reshape(sub_count, -1, partial_cols.shape[1])
    owner_sums = exchange_sum(by_group, "sub", sub_count, sub_index)
    owner_sums = owner_sums.reshape(head_count, -1, partial_cols.shape[1])
    owner_sums = exchange_sum(owner_sums, "head", head_count, lax.axis_index("head"))
    per_hs = req_count // hs_count
    out_block = partial_cols.shape[1]
    owner_sums = owner_sums.reshape(per_hs, local_rows, out_block)
    arrived_blocks = []
    for step in range(per_hs):
        chunk = lax.dynamic_index_in_dim(
            owner_sums, (req_index + step) % per_hs, axis=0, keepdims=False
        )
        pairs = []
        for c in range(req_count):
            for h in range(head_count):
                for u in range(sub_count):
                    j = u * head_count + h
                    k = j * per_hs + (c + step) % per_hs
                    src = c * hs_count + h * sub_count + u
                    pairs.append((src, k * hs_count + c // per_hs))
        arrived_blocks.append(lax.ppermute(chunk, ("req", "head", "sub"), pairs))
    stacked = jnp.stack(arrived_blocks)
    order = (req_index % per_hs - jnp.arange(per_hs)) % per_hs
    head_total = jnp.take(stacked, order, axis=0)
    head_total = jnp.transpose(head_total, (1, 0, 2)).reshape(local_rows, per_hs * out_block)
    head_total = head_total.astype(jnp.float32)
    out_width = head_total.shape[1]
    residual = lax.dynamic_slice_in_dim(hidden_in, hs_index * out_width, out_width, 1)
    return (residual.astype(jnp.float32) + head_total).astype(jnp.bfloat16)


def solution(mesh):
    in_specs = (
        P(("groups", "req"), None),
        P("req", ("head", "sub")),
        P(),
        P(("groups", "req"), None, "head"),
        P(("groups", "req"), None, "head"),
        P(("head", "sub"), "req"),
        P(("groups", "req")),
        P(("groups", "req")),
        P("groups"),
    )
    out_specs = P(("groups", "req"), ("head", "sub"))
    return jax.shard_map(local, mesh=mesh, in_specs=in_specs, out_specs=out_specs, check_vma=False)
```

profile of v0, /device:TPU:1, one launch (start us, length us, event | category | flops | bytes accessed | tf_op | source)
XLA Modules:
  0.0 288.7 jit_solution(2909639808181706036)
XLA Ops:
  6.5 3.2 %copy.35 = bf16[128,8192]{0,1:T(8,128)(2,1)S(1)} copy(bf16[128,8192]{1,0:T(8,128)(2,1)} %param.9) | data formatting | bytes 4194304 | tf_op args[0]
  9.9 0.5 copy.36
  10.4 30.1 %all_to_all.25 = bf16[128,4,1024]{2,0,1:T(8,128)(2,1)S(1)} all-to-all(bf16[128,4,1024]{2,0,1:T(8,128)(2,1)S(1)} %bitcast.76), channel_id=1, replica_groups=mesh['groups'=2,'req'=4,'head'=2,'sub'=2] {'req'}, dimensions={1} | all-to-all | bytes 2097152 | tf_op jit(solution)/shard_map/all_to_all | solution.py:49
  40.5 1.8 collective-permute-start
  42.7 1.9 collective-permute-done
  44.7 9.1 %convolution_convert_fusion.1 = bf16[512,2048]{1,0:T(8,128)(2,1)} fusion(bf16[512,2048]{1,0:T(8,128)(2,1)S(1)} %constant_dynamic-update-slice_fusion, bf16[2048,2048]{1,0:T(8,128)(2,1)} %param.10), kind=kOutput, calls=%fused_computation.11 | convolution fusion | flops 4296015872 | bytes 12582912 | tf_op jit(solution)/shard_map/dot_general | solution.py:63
  53.9 0.6 copy-done.3
  55.2 41.4 %reduce-scatter.2.cloned.1.call-done = bf16[128,2048]{1,0:T(8,128)(2,1)} async-done(((bf16[512,2048]{1,0:T(8,128)(2,1)}), bf16[128,2048]{1,0:T(8,128)(2,1)}) %reduce-scatter.2.cloned.1.call-update) | async-done | bytes 524304 | tf_op jit(solution)/shard_map/reduce_scatter | solution.py:62
  96.5 1.1 fusion.13
  97.9 0.3 reduce_sum.38
  98.8 1.6 convolution_convert_fusion.2
  100.4 3.5 %all-to-all-start.1 = ((bf16[4,64,2048]{2,1,0:T(8,128)(2,1)}), bf16[4,64,2048]{2,1,0:T(8,128)(2,1)S(1)}, u32[]{:S(2)}, u32[]{:S(2)}) async-start(bf16[4,64,2048]{2,1,0:T(8,128)(2,1)} %bitcast.12), calls=%async_computation.2 | async-start | bytes 2097152 | tf_op jit(solution)/shard_map/all_to_all | solution.py:95
  104.1 1.5 constant_dynamic-slice_fusion.1
  105.6 1.4 copy.34
  107.0 0.7 copy.33
  107.7 21.4 %all-to-all-done.1 = bf16[4,64,2048]{2,1,0:T(8,128)(2,1)S(1)} async-done(((bf16[4,64,2048]{2,1,0:T(8,128)(2,1)}), bf16[4,64,2048]{2,1,0:T(8,128)(2,1)S(1)}, u32[]{:S(2)}, u32[]{:S(2)}) %all-to-all-start.1) | async-done | bytes 1048608 | tf_op jit(solution)/shard_map/all_to_all | solution.py:95
  129.3 14.5 %fusion.36 = (f32[2,8,256]{2,1,0:T(8,128)S(1)}, f32[2,8,256,1601]{2,3,1,0:T(8,128)}) fusion(bf16[1601,2,128,1]{0,2,3,1:T(8,128)(2,1)} %bitcast.81, bf16[256,2,8,128]{3,2,1,0:T(8,128)(2,1)S(1)} %bitcast.79), kind=kOutput, calls=%fused_computation.54 | convolution fusion | flops 1698444800 | bytes 28115456 | tf_op jit(solution)/shard_map/sub | solution.py:104
  143.8 11.1 %fusion.12 = bf16[256,2,8,128]{0,3,2,1:T(8,128)(2,1)S(1)} fusion(bf16[1601,2,128,1]{0,2,3,1:T(8,128)(2,1)S(1)} %bitcast.80, f32[2,8,256,1601]{2,3,1,0:T(8,128)} %get-tuple-element.6, f32[2,8,256]{2,1,0:T(8,128)S(1)} %get-tuple-element.5), kind=kOutput, calls=%fused_computation.17 | convolution fusion | flops 1692409856 | bytes 28115456 | tf_op jit(solution)/shard_map/kgmt,tkd->mkgd/dot_general | solution.py:106
  154.9 1.1 copy.42
  156.0 0.5 reshape.85
  156.5 27.3 %all_to_all.26 = bf16[4,64,2048]{2,1,0:T(8,128)(2,1)S(1)} all-to-all(bf16[4,64,2048]{2,1,0:T(8,128)(2,1)S(1)} %reshape.85), channel_id=1, replica_groups=mesh['groups'=2,'req'=4,'head'=2,'sub'=2] {'req'}, dimensions={0} | all-to-all | bytes 2097152 | tf_op jit(solution)/shard_map/all_to_all | solution.py:110
  183.8 1.1 convolution_convert_fusion.3
  185.0 46.3 %all-gather.2.cloned.1.call-done = bf16[512,2048]{1,0:T(8,128)(2,1)} async-done(((bf16[128,2048]{1,0:T(8,128)(2,1)}), bf16[512,2048]{1,0:T(8,128)(2,1)}) %all-gather.2.cloned.1.call-update) | async-done | bytes 2097168 | tf_op jit(solution)/shard_map/all_gather | solution.py:118
  231.3 8.5 %convolution_convert_fusion = bf16[512,2048]{1,0:T(8,128)(2,1)S(1)} fusion(bf16[512,2048]{1,0:T(8,128)(2,1)} %all-gather.2.cloned.1.call-done, bf16[2048,2048]{1,0:T(8,128)(2,1)} %param.14), kind=kOutput, calls=%fused_computation.10 | convolution fusion | flops 4296015872 | bytes 12582912 | tf_op jit(solution)/shard_map/dot_general | solution.py:117
  239.9 0.7 collective-permute-start.1
  240.7 2.4 collective-permute-done.1
  243.1 1.6 fusion.10
  244.8 1.3 collective-permute-start.2
  246.0 11.9 %collective-permute-done.2 = bf16[128,2048]{1,0:T(8,128)(2,1)S(1)} collective-permute-done((bf16[128,2048]{1,0:T(8,128)(2,1)S(1)}, bf16[128,2048]{1,0:T(8,128)(2,1)S(1)}, u32[]{:S(2)}, u32[]{:S(2)}) %collective-permute-start.2) | collective-permute-done | bytes 524320 | tf_op jit(solution)/shard_map/ppermute | solution.py:21
  258.1 3.8 %collective-permute-start.3 = (bf16[128,2048]{1,0:T(8,128)(2,1)S(1)}, bf16[128,2048]{1,0:T(8,128)(2,1)S(1)}, u32[]{:S(2)}, u32[]{:S(2)}) collective-permute-start(bf16[128,2048]{1,0:T(8,128)(2,1)S(1)} %fusion.16), channel_id=1, source_target_pairs={{0,0},{1,8},{2,4},{3,12},{4,1},{5,9},{6,5},{7,13},{8,2},{9,10},{10... | collective-permute-start | bytes 1572872 | tf_op jit(solution)/shard_map/ppermute | solution.py:146
  261.9 18.0 %collective-permute-done.3 = bf16[128,2048]{1,0:T(8,128)(2,1)S(1)} collective-permute-done((bf16[128,2048]{1,0:T(8,128)(2,1)S(1)}, bf16[128,2048]{1,0:T(8,128)(2,1)S(1)}, u32[]{:S(2)}, u32[]{:S(2)}) %collective-permute-start.3) | collective-permute-done | bytes 524320 | tf_op jit(solution)/shard_map/ppermute | solution.py:146
  279.8 2.0 add_convert_fusion
  (35 shorter events, 2.7 us)
Async XLA Ops:
  6.5 48.6 %copy-start = (f32[128]{0:T(128)S(1)}, f32[128]{0:T(128)}, u32[]{:S(2)}) copy-start(f32[128]{0:T(128)} %param.11) | copy-start | bytes 1540
  6.5 90.0 %reduce-scatter.2.cloned.1.call-start = ((), (), s32[]{:S(2)}) async-start(), calls=%async_computation.4 | async-start | bytes 2621440 | tf_op jit(solution)/shard_map/reduce_scatter | solution.py:62
  40.5 4.1 %collective-permute-start = (bf16[512,1024]{1,0:T(8,128)(2,1)S(1)}, bf16[512,1024]{1,0:T(8,128)(2,1)S(1)}, u32[]{:S(2)}, u32[]{:S(2)}) collective-permute-start(bf16[512,1024]{1,0:T(8,128)(2,1)S(1)} %bitcast.69), channel_id=1, source_target_pairs={{0,1},{1,0},{2,3},{3,2},{4,5},{5,4},{6,7},{7,6},{8,9},{9,8},{10,11... | collective-permute-start | bytes 3145736 | tf_op jit(solution)/shard_map/ppermute | solution.py:56
  53.8 0.7 copy-start.3
  53.8 0.7 copy-start.4
  53.8 0.8 copy-start.5
  97.7 1.1 copy-start.2
  100.4 28.7 %all-to-all-start.1 = ((bf16[4,64,2048]{2,1,0:T(8,128)(2,1)}), bf16[4,64,2048]{2,1,0:T(8,128)(2,1)S(1)}, u32[]{:S(2)}, u32[]{:S(2)}) async-start(bf16[4,64,2048]{2,1,0:T(8,128)(2,1)} %bitcast.12), calls=%async_computation.2 | async-start | bytes 2097152 | tf_op jit(solution)/shard_map/all_to_all | solution.py:95
  103.9 127.4 %all-gather.2.cloned.1.call-start = ((), (), s32[]{:S(2)}) async-start(), calls=%async_computation.5 | async-start | bytes 2621440 | tf_op jit(solution)/shard_map/all_gather | solution.py:118
  239.9 3.2 %collective-permute-start.1 = (bf16[256,2048]{1,0:T(8,128)(2,1)S(1)}, bf16[256,2048]{1,0:T(8,128)(2,1)}, u32[]{:S(2)}, u32[]{:S(2)}) collective-permute-start(bf16[256,2048]{1,0:T(8,128)(2,1)S(1)} %dynamic-slice_bitcast_fusion), channel_id=1, source_target_pairs={{0,1},{1,0},{2,3},{3,2},{4,5},{5,4},{6,7},{7,6},{8,9},{9,8},{10,11... | collective-permute-start | bytes 3145736 | tf_op jit(solution)/shard_map/ppermute | solution.py:21
  244.7 37.2 %copy-start.1 = (f32[128]{0:T(128)S(1)}, f32[128]{0:T(128)}, u32[]{:S(2)}) copy-start(f32[128]{0:T(128)} %param.11) | copy-start | bytes 1540
  244.8 13.2 %collective-permute-start.2 = (bf16[128,2048]{1,0:T(8,128)(2,1)S(1)}, bf16[128,2048]{1,0:T(8,128)(2,1)S(1)}, u32[]{:S(2)}, u32[]{:S(2)}) collective-permute-start(bf16[128,2048]{1,0:T(8,128)(2,1)S(1)} %dynamic-slice_bitcast_fusion.1), channel_id=1, source_target_pairs={{0,2},{2,0},{1,3},{3,1},{4,6},{6,4},{5,7},{7,5},{8,10},{10,8},{9,1... | collective-permute-start | bytes 1572872 | tf_op jit(solution)/shard_map/ppermute | solution.py:21
  258.1 21.7 %collective-permute-start.3 = (bf16[128,2048]{1,0:T(8,128)(2,1)S(1)}, bf16[128,2048]{1,0:T(8,128)(2,1)S(1)}, u32[]{:S(2)}, u32[]{:S(2)}) collective-permute-start(bf16[128,2048]{1,0:T(8,128)(2,1)S(1)} %fusion.16), channel_id=1, source_target_pairs={{0,0},{1,8},{2,4},{3,12},{4,1},{5,9},{6,5},{7,13},{8,2},{9,10},{10... | collective-permute-start | bytes 1572872 | tf_op jit(solution)/shard_map/ppermute | solution.py:146
Sparse Core Ops, SparseCore 0:
  54.0 42.5 reduce-scatter.1
  185.1 46.1 all-gather.1
where the time goes:
time: 289 us
  waiting for transfers between devices  143 us (49%)
  blocking collectives  57.4 us (20%)
  matrix products  46 us (16%)
  between operations  13.7 us (5%)
  starting transfers between devices  11.3 us (4%)
  local copies, waits for them, and re-layouts  11.2 us (4%)
  other arithmetic  5.88 us (2%)
    all_gather x1, waiting for transfers between devices, local(): lax.all_gather(attended, 'req', axis=0, tiled=True)  46.3 us
    reduce_scatter x1, waiting for transfers between devices, local(): lax.psum_scatter(jnp.dot(spread_cols, q_weight, preferred_element_type=jn...  41.4 us
    all_to_all x1, blocking collectives, local(): lax.all_to_all(my_part, 'req', split_axis=1, concat_axis=0, tiled=True)  30.1 us
    all_to_all x1, blocking collectives, local(): lax.all_to_all(replies, 'req', split_axis=0, concat_axis=0, tiled=True)  27.3 us
    all_to_all x1, waiting for transfers between devices, local(): lax.all_to_all(outgoing, 'req', split_axis=0, concat_axis=0, tiled=True)  21.4 us
    ppermute x1, waiting for transfers between devices, local(): arrived_blocks.append(lax.ppermute(chunk, ('req', 'head', 'sub'), pairs))  18 us
    sub x1, matrix products, local(): weights = jnp.exp(scores - row_peak)  14.5 us
    ppermute x2, waiting for transfers between devices, exchange_sum(): lax.ppermute(outgoing, axis, [(i, (i + shift) % count) for i in range(cou...  14.4 us
  transfers between devices with their start and end apart: 7, of which 7 were waited for; matrix products, arithmetic and copies ran while one was open for 2% of the time, Pallas kernels for 0%

commit v1 on v0

--- a/solution.py
+++ b/solution.py
@@ -5,6 +5,27 @@
 
 HQ = 64
 KVH = 8
+
+
+def ring_gather(x, axis, dim):
+    length, index, rows = (lax.axis_size(axis), lax.axis_index(axis), x.shape[dim])
+    ahead = [(i, (i + 1) % length) for i in range(length)]
+    backward = [(i, (i - 1) % length) for i in range(length)]
+    result = jnp.zeros((*x.shape[:dim], length * rows, *x.shape[dim + 1 :]), x.dtype)
+    result = lax.dynamic_update_slice_in_dim(result, x, index * rows, axis=dim)
+    from_left = from_right = x
+    middle = length // 2
+    for hop in range(1, middle + 1):
+        from_left = lax.ppermute(from_left, axis, ahead)
+        result = lax.dynamic_update_slice_in_dim(
+            result, from_left, (index - hop) % length * rows, axis=dim
+        )
+        if hop < length - middle:
+            from_right = lax.ppermute(from_right, axis, backward)
+            result = lax.dynamic_update_slice_in_dim(
+                result, from_right, (index + hop) % length * rows, axis=dim
+            )
+    return result
 
 
 def normalize_heads(queries, q_gain, head_dim):
@@ -115,9 +136,7 @@
         preferred_element_type=jnp.float32,
     ).astype(jnp.bfloat16)
     partial_cols = jnp.dot(
-        lax.all_gather(attended, "req", axis=0, tiled=True),
-        out_weight,
-        preferred_element_type=jnp.float32,
+        ring_gather(attended, "req", 0), out_weight, preferred_element_type=jnp.float32
     ).astype(jnp.bfloat16)
     hs_count = lax.axis_size("head") * sub_count
     hs_index = lax.axis_index("head") * sub_count + sub_index

time: 289 us -> 286 us (0.990)
  blocking collectives: 57.4 us -> 30.1 us
  waiting for transfers between devices: 143 us -> 155 us
  starting transfers between devices: 11.3 us -> 17.9 us
  local copies, waits for them, and re-layouts: 11.2 us -> 16 us
    all_gather x1 -> x0, waiting for transfers between devices: 46.3 us -> none  [local(): lax.all_gather(attended, 'req', axis=0, tiled=True)]
    ppermute x0 -> x3, waiting for transfers between devices: none -> 31.4 us  [the longest x2 22.8 us: ring_gather(): from_left = lax.ppermute(from_left, axis, ahead)]
    all_to_all x1 -> x0, blocking collectives: 27.3 us -> none  [local(): lax.all_to_all(replies, 'req', split_axis=0, concat_axis=0, tiled=True)]
    all_to_all x0 -> x1, waiting for transfers between devices: none -> 25.2 us  [local(): lax.all_to_all(replies, 'req', split_axis=0, concat_axis=0, tiled=True)]
    all_to_all x0 -> x1, starting transfers between devices: none -> 3.51 us  [local(): lax.all_to_all(replies, 'req', split_axis=0, concat_axis=0, tiled=True)]
    ppermute x0 -> x3, starting transfers between devices: none -> 3.27 us  [the longest x1 3.26 us: ring_gather(): from_right = lax.ppermute(from_right, axis, backward)]
  transfers between devices with their start and end apart: 7 -> 10, of which waited for: 7 -> 10; matrix products, arithmetic and copies ran while one was open for 2% -> 2% of each run, Pallas kernels for 0% -> 0%
where the time goes in v1:
time: 286 us; the launch traced here: 285 us
  waiting for transfers between devices  155 us (54%)
  matrix products  46 us (16%)
  blocking collectives  30.1 us (11%)
  starting transfers between devices  17.9 us (6%)
  local copies, waits for them, and re-layouts  16 us (6%)
  between operations  13.7 us (5%)
  other arithmetic  5.88 us (2%)
    reduce_scatter x1, waiting for transfers between devices, local(): lax.psum_scatter(jnp.dot(spread_cols, q_weight, preferred_element_type=jn...  41.4 us
    all_to_all x1, blocking collectives, local(): lax.all_to_all(my_part, 'req', split_axis=1, concat_axis=0, tiled=True)  30.1 us
    all_to_all x1, waiting for transfers between devices, local(): lax.all_to_all(replies, 'req', split_axis=0, concat_axis=0, tiled=True)  25.2 us
    ppermute x2, waiting for transfers between devices, ring_gather(): from_left = lax.ppermute(from_left, axis, ahead)  22.8 us
    all_to_all x1, waiting for transfers between devices, local(): lax.all_to_all(outgoing, 'req', split_axis=0, concat_axis=0, tiled=True)  21.5 us
    ppermute x1, waiting for transfers between devices, local(): arrived_blocks.append(lax.ppermute(chunk, ('req', 'head', 'sub'), pairs))  19.8 us
    sub x1, matrix products, local(): weights = jnp.exp(scores - row_peak)  14.6 us
    ppermute x2, waiting for transfers between devices, exchange_sum(): lax.ppermute(outgoing, axis, [(i, (i + shift) % count) for i in range(cou...  14.4 us
  transfers between devices with their start and end apart: 10, of which 10 were waited for; matrix products, arithmetic and copies ran while one was open for 2% of the time, Pallas kernels for 0%

profile of v1, /device:TPU:1, one launch (start us, length us, event | category | flops | bytes accessed | tf_op | source)
XLA Modules:
  0.0 285.0 jit_solution(14634861111898528705)
XLA Ops:
  6.5 3.2 %copy.35 = bf16[128,8192]{0,1:T(8,128)(2,1)S(1)} copy(bf16[128,8192]{1,0:T(8,128)(2,1)} %param.9) | data formatting | bytes 4194304 | tf_op args[0]
  10.4 30.1 %all_to_all.25 = bf16[128,4,1024]{2,0,1:T(8,128)(2,1)S(1)} all-to-all(bf16[128,4,1024]{2,0,1:T(8,128)(2,1)S(1)} %bitcast.76), channel_id=1, replica_groups=mesh['groups'=2,'req'=4,'head'=2,'sub'=2] {'req'}, dimensions={1} | all-to-all | bytes 2097152 | tf_op jit(solution)/shard_map/all_to_all | solution.py:70
  40.5 1.8 collective-permute-start
  42.7 1.9 collective-permute-done
  44.7 9.1 %convolution_convert_fusion.1 = bf16[512,2048]{1,0:T(8,128)(2,1)} fusion(bf16[512,2048]{1,0:T(8,128)(2,1)S(1)} %constant_dynamic-update-slice_fusion.4, bf16[2048,2048]{1,0:T(8,128)(2,1)} %param.10), kind=kOutput, calls=%fused_computation.11 | convolution fusion | flops 4296015872 | bytes 12582912 | tf_op jit(solution)/shard_map/dot_general | solution.py:84
  55.2 41.4 %reduce-scatter.2.cloned.1.call-done = bf16[128,2048]{1,0:T(8,128)(2,1)} async-done(((bf16[512,2048]{1,0:T(8,128)(2,1)}), bf16[128,2048]{1,0:T(8,128)(2,1)}) %reduce-scatter.2.cloned.1.call-update) | async-done | bytes 524304 | tf_op jit(solution)/shard_map/reduce_scatter | solution.py:83
  96.5 1.1 fusion.13
  98.8 1.6 convolution_convert_fusion.2
  100.3 3.7 %all-to-all-start.1 = ((bf16[4,64,2048]{2,1,0:T(8,128)(2,1)}), bf16[4,64,2048]{2,1,0:T(8,128)(2,1)S(1)}, u32[]{:S(2)}, u32[]{:S(2)}) async-start(bf16[4,64,2048]{2,1,0:T(8,128)(2,1)} %bitcast.12), calls=%async_computation.2 | async-start | bytes 2097152 | tf_op jit(solution)/shard_map/all_to_all | solution.py:116
  104.1 1.5 constant_dynamic-slice_fusion.1
  105.6 1.4 copy.34
  107.6 21.5 %all-to-all-done.1 = bf16[4,64,2048]{2,1,0:T(8,128)(2,1)S(1)} async-done(((bf16[4,64,2048]{2,1,0:T(8,128)(2,1)}), bf16[4,64,2048]{2,1,0:T(8,128)(2,1)S(1)}, u32[]{:S(2)}, u32[]{:S(2)}) %all-to-all-start.1) | async-done | bytes 1048608 | tf_op jit(solution)/shard_map/all_to_all | solution.py:116
  129.3 14.6 %fusion.36 = (f32[2,8,256]{2,1,0:T(8,128)S(1)}, f32[2,8,256,1601]{2,3,1,0:T(8,128)}) fusion(bf16[1601,2,128,1]{0,2,3,1:T(8,128)(2,1)} %bitcast.81, bf16[256,2,8,128]{3,2,1,0:T(8,128)(2,1)S(1)} %bitcast.79), kind=kOutput, calls=%fused_computation.58 | convolution fusion | flops 1698444800 | bytes 28115456 | tf_op jit(solution)/shard_map/sub | solution.py:125
  143.8 11.1 %fusion.12 = bf16[256,2,8,128]{0,3,2,1:T(8,128)(2,1)S(1)} fusion(bf16[1601,2,128,1]{0,2,3,1:T(8,128)(2,1)S(1)} %bitcast.80, f32[2,8,256,1601]{2,3,1,0:T(8,128)} %get-tuple-element.6, f32[2,8,256]{2,1,0:T(8,128)S(1)} %get-tuple-element.5), kind=kOutput, calls=%fused_computation.17 | convolution fusion | flops 1692409856 | bytes 28115456 | tf_op jit(solution)/shard_map/kgmt,tkd->mkgd/dot_general | solution.py:127
  156.0 1.3 reshape.85
  157.3 3.5 %all-to-all-start.2 = ((bf16[4,64,2048]{2,1,0:T(8,128)(2,1)}), bf16[4,64,2048]{2,1,0:T(8,128)(2,1)S(1)}, u32[]{:S(2)}, u32[]{:S(2)}) async-start(bf16[4,64,2048]{2,1,0:T(8,128)(2,1)} %reshape.85), calls=%async_computation.3 | async-start | bytes 2097152 | tf_op jit(solution)/shard_map/all_to_all | solution.py:131
  160.8 25.2 %all-to-all-done.2 = bf16[4,64,2048]{2,1,0:T(8,128)(2,1)S(1)} async-done(((bf16[4,64,2048]{2,1,0:T(8,128)(2,1)}), bf16[4,64,2048]{2,1,0:T(8,128)(2,1)S(1)}, u32[]{:S(2)}, u32[]{:S(2)}) %all-to-all-start.2) | async-done | bytes 1048608 | tf_op jit(solution)/shard_map/all_to_all | solution.py:131
  186.0 1.6 broadcast.49
  187.6 1.1 constant_dynamic-update-slice_fusion.3
  188.8 3.3 %collective-permute-start.2 = (bf16[128,2048]{1,0:T(8,128)(2,1)S(1)}, bf16[128,2048]{1,0:T(8,128)(2,1)S(1)}, u32[]{:S(2)}, u32[]{:S(2)}) collective-permute-start(bf16[128,2048]{1,0:T(8,128)(2,1)S(1)} %get-tuple-element.8), channel_id=1, source_target_pairs={{0,12},{4,0},{8,4},{12,8},{1,13},{5,1},{9,5},{13,9},{2,14},{6,2},{... | collective-permute-start | bytes 1572872 | tf_op jit(solution)/shard_map/ppermute | solution.py:24
  192.0 10.6 %collective-permute-done.1 = bf16[128,2048]{1,0:T(8,128)(2,1)S(1)} collective-permute-done((bf16[128,2048]{1,0:T(8,128)(2,1)S(1)}, bf16[128,2048]{1,0:T(8,128)(2,1)S(1)}, u32[]{:S(2)}, u32[]{:S(2)}) %collective-permute-start.1) | collective-permute-done | bytes 524320 | tf_op jit(solution)/shard_map/ppermute | solution.py:19
  203.4 8.5 %collective-permute-done.2 = bf16[128,2048]{1,0:T(8,128)(2,1)S(1)} collective-permute-done((bf16[128,2048]{1,0:T(8,128)(2,1)S(1)}, bf16[128,2048]{1,0:T(8,128)(2,1)S(1)}, u32[]{:S(2)}, u32[]{:S(2)}) %collective-permute-start.2) | collective-permute-done | bytes 524320 | tf_op jit(solution)/shard_map/ppermute | solution.py:24
  212.8 12.3 %collective-permute-done.3 = bf16[128,2048]{1,0:T(8,128)(2,1)S(1)} collective-permute-done((bf16[128,2048]{1,0:T(8,128)(2,1)S(1)}, bf16[128,2048]{1,0:T(8,128)(2,1)S(1)}, u32[]{:S(2)}, u32[]{:S(2)}) %collective-permute-start.3) | collective-permute-done | bytes 524320 | tf_op jit(solution)/shard_map/ppermute | solution.py:19
  225.9 8.5 %convolution_convert_fusion = bf16[512,2048]{1,0:T(8,128)(2,1)S(1)} fusion(bf16[512,2048]{1,0:T(8,128)(2,1)} %constant_dynamic-update-slice_fusion, bf16[2048,2048]{1,0:T(8,128)(2,1)} %param.14), kind=kOutput, calls=%fused_computation.10 | convolution fusion | flops 4296015872 | bytes 12582912 | tf_op jit(solution)/shard_map/dot_general | solution.py:138
  234.5 2.4 collective-permute-start.4
  236.9 2.4 collective-permute-done.4
  239.4 1.6 fusion.10
  241.0 1.2 collective-permute-start.5
  242.3 12.0 %collective-permute-done.5 = bf16[128,2048]{1,0:T(8,128)(2,1)S(1)} collective-permute-done((bf16[128,2048]{1,0:T(8,128)(2,1)S(1)}, bf16[128,2048]{1,0:T(8,128)(2,1)S(1)}, u32[]{:S(2)}, u32[]{:S(2)}) %collective-permute-start.5) | collective-permute-done | bytes 524320 | tf_op jit(solution)/shard_map/ppermute | solution.py:42
  254.4 1.9 collective-permute-start.6
  256.3 19.8 %collective-permute-done.6 = bf16[128,2048]{1,0:T(8,128)(2,1)S(1)} collective-permute-done((bf16[128,2048]{1,0:T(8,128)(2,1)S(1)}, bf16[128,2048]{1,0:T(8,128)(2,1)S(1)}, u32[]{:S(2)}, u32[]{:S(2)}) %collective-permute-start.6) | collective-permute-done | bytes 524320 | tf_op jit(solution)/shard_map/ppermute | solution.py:165
  276.1 2.0 add_convert_fusion
  (43 shorter events, 8.2 us)
Async XLA Ops:
  6.5 48.6 %copy-start = (f32[128]{0:T(128)S(1)}, f32[128]{0:T(128)}, u32[]{:S(2)}) copy-start(f32[128]{0:T(128)} %param.11) | copy-start | bytes 1540
  6.5 90.0 %reduce-scatter.2.cloned.1.call-start = ((), (), s32[]{:S(2)}) async-start(), calls=%async_computation.4 | async-start | bytes 2621440 | tf_op jit(solution)/shard_map/reduce_scatter | solution.py:83
  40.5 4.1 %collective-permute-start = (bf16[512,1024]{1,0:T(8,128)(2,1)S(1)}, bf16[512,1024]{1,0:T(8,128)(2,1)S(1)}, u32[]{:S(2)}, u32[]{:S(2)}) collective-permute-start(bf16[512,1024]{1,0:T(8,128)(2,1)S(1)} %bitcast.69), channel_id=1, source_target_pairs={{0,1},{1,0},{2,3},{3,2},{4,5},{5,4},{6,7},{7,6},{8,9},{9,8},{10,11... | collective-permute-start | bytes 3145736 | tf_op jit(solution)/shard_map/ppermute | solution.py:77
  53.8 0.7 copy-start.3
  53.8 0.7 copy-start.4
  53.8 0.8 copy-start.5
  97.7 1.1 copy-start.2
  100.3 28.7 %all-to-all-start.1 = ((bf16[4,64,2048]{2,1,0:T(8,128)(2,1)}), bf16[4,64,2048]{2,1,0:T(8,128)(2,1)S(1)}, u32[]{:S(2)}, u32[]{:S(2)}) async-start(bf16[4,64,2048]{2,1,0:T(8,128)(2,1)} %bitcast.12), calls=%async_computation.2 | async-start | bytes 2097152 | tf_op jit(solution)/shard_map/all_to_all | solution.py:116
  157.3 28.7 %all-to-all-start.2 = ((bf16[4,64,2048]{2,1,0:T(8,128)(2,1)}), bf16[4,64,2048]{2,1,0:T(8,128)(2,1)S(1)}, u32[]{:S(2)}, u32[]{:S(2)}) async-start(bf16[4,64,2048]{2,1,0:T(8,128)(2,1)} %reshape.85), calls=%async_computation.3 | async-start | bytes 2097152 | tf_op jit(solution)/shard_map/all_to_all | solution.py:131
  188.8 13.8 %collective-permute-start.1 = (bf16[128,2048]{1,0:T(8,128)(2,1)S(1)}, bf16[128,2048]{1,0:T(8,128)(2,1)S(1)}, u32[]{:S(2)}, u32[]{:S(2)}) collective-permute-start(bf16[128,2048]{1,0:T(8,128)(2,1)S(1)} %get-tuple-element.8), channel_id=1, source_target_pairs={{0,4},{4,8},{8,12},{12,0},{1,5},{5,9},{9,13},{13,1},{2,6},{6,10},{... | collective-permute-start | bytes 1572872 | tf_op jit(solution)/shard_map/ppermute | solution.py:19
  188.8 23.2 %collective-permute-start.2 = (bf16[128,2048]{1,0:T(8,128)(2,1)S(1)}, bf16[128,2048]{1,0:T(8,128)(2,1)S(1)}, u32[]{:S(2)}, u32[]{:S(2)}) collective-permute-start(bf16[128,2048]{1,0:T(8,128)(2,1)S(1)} %get-tuple-element.8), channel_id=1, source_target_pairs={{0,12},{4,0},{8,4},{12,8},{1,13},{5,1},{9,5},{13,9},{2,14},{6,2},{... | collective-permute-start | bytes 1572872 | tf_op jit(solution)/shard_map/ppermute | solution.py:24
  202.6 22.5 %collective-permute-start.3 = (bf16[128,2048]{1,0:T(8,128)(2,1)S(1)}, bf16[128,2048]{1,0:T(8,128)(2,1)S(1)}, u32[]{:S(2)}, u32[]{:S(2)}) collective-permute-start(bf16[128,2048]{1,0:T(8,128)(2,1)S(1)} %collective-permute-done.1), channel_id=1, source_target_pairs={{0,4},{4,8},{8,12},{12,0},{1,5},{5,9},{9,13},{13,1},{2,6},{6,10},{... | collective-permute-start | bytes 1572872 | tf_op jit(solution)/shard_map/ppermute | solution.py:19
  234.5 4.8 %collective-permute-start.4 = (bf16[256,2048]{1,0:T(8,128)(2,1)S(1)}, bf16[256,2048]{1,0:T(8,128)(2,1)}, u32[]{:S(2)}, u32[]{:S(2)}) collective-permute-start(bf16[256,2048]{1,0:T(8,128)(2,1)S(1)} %dynamic-slice_bitcast_fusion), channel_id=1, source_target_pairs={{0,1},{1,0},{2,3},{3,2},{4,5},{5,4},{6,7},{7,6},{8,9},{9,8},{10,11... | collective-permute-start | bytes 3145736 | tf_op jit(solution)/shard_map/ppermute | solution.py:42
  241.0 37.2 %copy-start.1 = (f32[128]{0:T(128)S(1)}, f32[128]{0:T(128)}, u32[]{:S(2)}) copy-start(f32[128]{0:T(128)} %param.11) | copy-start | bytes 1540
  241.0 13.2 %collective-permute-start.5 = (bf16[128,2048]{1,0:T(8,128)(2,1)S(1)}, bf16[128,2048]{1,0:T(8,128)(2,1)S(1)}, u32[]{:S(2)}, u32[]{:S(2)}) collective-permute-start(bf16[128,2048]{1,0:T(8,128)(2,1)S(1)} %dynamic-slice_bitcast_fusion.1), channel_id=1, source_target_pairs={{0,2},{2,0},{1,3},{3,1},{4,6},{6,4},{5,7},{7,5},{8,10},{10,8},{9,1... | collective-permute-start | bytes 1572872 | tf_op jit(solution)/shard_map/ppermute | solution.py:42
  254.4 21.7 %collective-permute-start.6 = (bf16[128,2048]{1,0:T(8,128)(2,1)S(1)}, bf16[128,2048]{1,0:T(8,128)(2,1)S(1)}, u32[]{:S(2)}, u32[]{:S(2)}) collective-permute-start(bf16[128,2048]{1,0:T(8,128)(2,1)S(1)} %fusion.16), channel_id=1, source_target_pairs={{0,0},{1,8},{2,4},{3,12},{4,1},{5,9},{6,5},{7,13},{8,2},{9,10},{10... | collective-permute-start | bytes 1572872 | tf_op jit(solution)/shard_map/ppermute | solution.py:165
Sparse Core Ops, SparseCore 0:
  54.0 42.5 reduce-scatter.1
